TPU v7x, 32 devices: a whole 2x2x4 slice. The times are simulated.
32 devices in a mesh: shard: 8 (over z, x), tensor: 4 (over y, core).
Axes of the slice: x: 2, y: 2, z: 4, core: 2. Of those that a mesh axis runs over, the one named last changes fastest.
Arguments:
- wide_weight: bfloat16 [4, 4096, 4096], P(None, 'shard', 'tensor'), may hold values from -6 to 6
- wide_grad: bfloat16 [4, 4096, 4096], P(None, 'shard', 'tensor'), may hold values from -6 to 6
- wide_first: float32 [4, 4096, 256], P(None, ('shard', 'tensor')), may hold values from -4 to 4
- wide_second: float32 [4, 4096, 256], P(None, ('shard', 'tensor')), may hold values from 0.001 to 0.1
- wide_basis: bfloat16 [4, 4096, 256], P(None, 'tensor'), may hold values from -0.09375 to 0.09375
- narrow_weight: bfloat16 [4, 1024, 4096], P(None, 'shard', 'tensor'), may hold values from -6 to 6
- narrow_grad: bfloat16 [4, 1024, 4096], P(None, 'shard', 'tensor'), may hold values from -6 to 6
- narrow_first: float32 [4, 1024, 256], P(None, ('shard', 'tensor')), may hold values from -4 to 4
- narrow_second: float32 [4, 1024, 256], P(None, ('shard', 'tensor')), may hold values from 0.001 to 0.1
- narrow_basis: bfloat16 [4, 4096, 256], P(None, 'tensor'), may hold values from -0.09375 to 0.09375
- vocab_weight: bfloat16 [2, 32000, 4096], P(None, 'shard', 'tensor'), may hold values from -6 to 6
- vocab_grad: bfloat16 [2, 32000, 4096], P(None, 'shard', 'tensor'), may hold values from -6 to 6
- vocab_first: float32 [2, 32000, 256], P(None, ('shard', 'tensor')), may hold values from -4 to 4
- vocab_second: float32 [2, 32000, 256], P(None, ('shard', 'tensor')), may hold values from 0.001 to 0.1
- vocab_basis: bfloat16 [2, 4096, 256], P(None, 'tensor'), may hold values from -0.09375 to 0.09375
Outputs:
- wide_weight_new: bfloat16 [4, 4096, 4096], P(None, 'shard', 'tensor')
- wide_first_new: float32 [4, 4096, 256], P(None, ('shard', 'tensor'))
- wide_second_new: float32 [4, 4096, 256], P(None, ('shard', 'tensor'))
- narrow_weight_new: bfloat16 [4, 1024, 4096], P(None, 'shard', 'tensor')
- narrow_first_new: float32 [4, 1024, 256], P(None, ('shard', 'tensor'))
- narrow_second_new: float32 [4, 1024, 256], P(None, ('shard', 'tensor'))
- vocab_weight_new: bfloat16 [2, 32000, 4096], P(None, 'shard', 'tensor')
- vocab_first_new: float32 [2, 32000, 256], P(None, ('shard', 'tensor'))
- vocab_second_new: float32 [2, 32000, 256], P(None, ('shard', 'tensor'))
All inputs are finite; a program needn't handle non-finite values.
Results may differ from a plain program's by a relative error of at most 0.01.
Values may be sent and summed in bfloat16 or wider, within the bound.
No kernel may reach another device: no remote copies, remote signals or barrier semaphores. Data moves between devices by JAX's collectives and lax.ppermute only.
A program may use at most 192 MiB of HBM per device.

v0:
```python
import jax
import jax.numpy as jnp
from jax import lax
from jax.sharding import PartitionSpec as P

NS_ITERS = 3


HIGHEST = lax.Precision.HIGHEST


def local_gram(polish):
    return jnp.einsum("sdk,sdl->skl", polish, polish, precision=HIGHEST)


def polish_small(back, gram):
    trace = jnp.einsum("skk->s", gram)
    scale = 1.0 / jnp.sqrt(trace + 1e-06)
    small = gram * (scale * scale)[:, None, None]
    rank = gram.shape[1]
    eye = jnp.eye(rank, dtype=jnp.float32)[None, :, :]
    factor = jnp.broadcast_to(eye, gram.shape)
    for step in range(NS_ITERS):
        square = jnp.einsum("skl,slm->skm", small, small, precision=HIGHEST)
        turn = 3.4445 * eye - 4.775 * small + 2.0315 * square
        factor = jnp.einsum("skl,slm->skm", factor, turn, precision=HIGHEST)
        if step + 1 < NS_ITERS:
            small = jnp.einsum(
                "skl,slm->skm",
                turn,
                jnp.einsum("skl,slm->skm", small, turn, precision=HIGHEST),
                precision=HIGHEST,
            )
    return jnp.einsum("sdk,skl->sdl", back * scale[:, None, None], factor, precision=HIGHEST)


def adam_moments(first, second, projected):
    first_new = 0.9 * first + 0.1 * projected
    second_new = 0.999 * second + 0.001 * projected * projected
    direction = first_new / (1.0 - 0.9**10) / (jnp.sqrt(second_new / (1.0 - 0.999**10)) + 1e-08)
    return (first_new, second_new, direction.astype(jnp.bfloat16))


def per_device(
    wide_weight,
    wide_grad,
    wide_first,
    wide_second,
    wide_basis,
    narrow_weight,
    narrow_grad,
    narrow_first,
    narrow_second,
    narrow_basis,
    vocab_weight,
    vocab_grad,
    vocab_first,
    vocab_second,
    vocab_basis,
):
    weights = (wide_weight, narrow_weight, vocab_weight)
    grads = (wide_grad, narrow_grad, vocab_grad)
    firsts = (wide_first, narrow_first, vocab_first)
    seconds = (wide_second, narrow_second, vocab_second)
    olds = (wide_basis, narrow_basis, vocab_basis)
    sketch_terms = [
        jnp.einsum("smc,scr->smr", grad, old, preferred_element_type=jnp.float32)
        for grad, old in zip(grads, olds)
    ]
    sketch_sum = (
        lax.psum(sketch_terms[0].astype(jnp.bfloat16), "tensor").astype(jnp.float32),
        lax.psum(sketch_terms[1].astype(jnp.bfloat16), "tensor").astype(jnp.float32),
        lax.psum(sketch_terms[2].astype(jnp.bfloat16), "tensor").astype(jnp.float32),
    )
    sketches = [item.astype(jnp.bfloat16) for item in sketch_sum]
    back_terms = [
        jnp.einsum("smc,smr->scr", grad, sketch, preferred_element_type=jnp.float32)
        for grad, sketch in zip(grads, sketches)
    ]
    backs = (
        lax.psum_scatter(back_terms[0], "shard", scatter_dimension=1, tiled=True),
        lax.psum_scatter(back_terms[1], "shard", scatter_dimension=1, tiled=True),
        lax.psum_scatter(back_terms[2], "shard", scatter_dimension=1, tiled=True),
    )
    first_grams = lax.psum(tuple((local_gram(back) for back in backs)), ("shard", "tensor"))
    rounded = [
        polish_small(back, gram).astype(jnp.bfloat16) for back, gram in zip(backs, first_grams)
    ]
    bases = (
        lax.all_gather(rounded[0], "shard", axis=1, tiled=True),
        lax.all_gather(rounded[1], "shard", axis=1, tiled=True),
        lax.all_gather(rounded[2], "shard", axis=1, tiled=True),
    )
    proj_terms = [
        jnp.einsum("smc,scr->smr", grad, basis, preferred_element_type=jnp.float32)
        for grad, basis in zip(grads, bases)
    ]
    projected = (
        lax.psum_scatter(proj_terms[0], "tensor", scatter_dimension=1, tiled=True),
        lax.psum_scatter(proj_terms[1], "tensor", scatter_dimension=1, tiled=True),
        lax.psum_scatter(proj_terms[2], "tensor", scatter_dimension=1, tiled=True),
    )
    results = [
        adam_moments(first, second, proj) for first, second, proj in zip(firsts, seconds, projected)
    ]
    directions = (
        lax.all_gather(results[0][2], "tensor", axis=1, tiled=True),
        lax.all_gather(results[1][2], "tensor", axis=1, tiled=True),
        lax.all_gather(results[2][2], "tensor", axis=1, tiled=True),
    )
    outputs = []
    for weight, direction, basis, result in zip(weights, directions, bases, results):
        update = jnp.einsum("smr,scr->smc", direction, basis, preferred_element_type=jnp.float32)
        weight_new = (0.99 * weight.astype(jnp.float32) - 2.0 * update).astype(jnp.bfloat16)
        outputs.append((weight_new, result[0], result[1]))
    return (
        outputs[0][0],
        outputs[0][1],
        outputs[0][2],
        outputs[1][0],
        outputs[1][1],
        outputs[1][2],
        outputs[2][0],
        outputs[2][1],
        outputs[2][2],
    )


def solution(mesh):
    in_specs = (
        P(None, "shard", "tensor"),
        P(None, "shard", "tensor"),
        P(None, ("shard", "tensor"), None),
        P(None, ("shard", "tensor"), None),
        P(None, "tensor", None),
        P(None, "shard", "tensor"),
        P(None, "shard", "tensor"),
        P(None, ("shard", "tensor"), None),
        P(None, ("shard", "tensor"), None),
        P(None, "tensor", None),
        P(None, "shard", "tensor"),
        P(None, "shard", "tensor"),
        P(None, ("shard", "tensor"), None),
        P(None, ("shard", "tensor"), None),
        P(None, "tensor", None),
    )
    out_specs = (
        P(None, "shard", "tensor"),
        P(None, ("shard", "tensor"), None),
        P(None, ("shard", "tensor"), None),
        P(None, "shard", "tensor"),
        P(None, ("shard", "tensor"), None),
        P(None, ("shard", "tensor"), None),
        P(None, "shard", "tensor"),
        P(None, ("shard", "tensor"), None),
        P(None, ("shard", "tensor"), None),
    )
    return jax.shard_map(
        per_device, mesh=mesh, in_specs=in_specs, out_specs=out_specs, check_vma=False
    )
```

profile of v0, /device:TPU:0, one launch (start us, length us, event | category | flops | bytes accessed | tf_op | source)
XLA Modules:
  0.0 922.7 jit_solution(10910709305503595160)
XLA Ops:
  7.2 12.4 %convolution_convert_fusion = bf16[2,4000,256]{2,1,0:T(8,128)(2,1)} fusion(bf16[2,4000,1024]{2,1,0:T(8,128)(2,1)} %param.26, bf16[2,1024,256]{2,1,0:T(8,128)(2,1)} %param.29), kind=kOutput, calls=%fused_computation.3 | convolution fusion | flops 4196352000 | bytes 21528576 | tf_op jit(solution)/shard_map/smc,scr->smr/dot_general | solution.py:67
  19.7 4.6 convolution_convert_fusion.1
  26.0 108.4 %all-reduce.11.cloned.1.call-done = (bf16[4,512,256]{1,2,0:T(8,128)(2,1)}, bf16[4,128,256]{1,2,0:T(8,128)(2,1)}, bf16[2,4000,256]{2,1,0:T(8,128)(2,1)}) async-done(((bf16[4,512,256]{1,2,0:T(8,128)(2,1)}, bf16[4,128,256]{1,2,0:T(8,128)(2,1)}, bf16[2,4000,256]{2,1,0:T(8,128)(2,1)}), (bf16[4,512,256]{1,2,0:T(8,128)(2,1)}, bf16[4,128,256]{1,2,0:T(8,128)(2,1)}, ...) | async-done | bytes 5406736 | tf_op jit(solution)/shard_map/psum | solution.py:71
  134.3 12.8 %convolution_bitcast_fusion.3 = f32[2,1024,256]{1,2,0:T(8,128)} fusion(bf16[2,4000,256]{2,1,0:T(8,128)(2,1)} %get-tuple-element.34, bf16[2,4000,1024]{2,1,0:T(8,128)(2,1)} %param.26), kind=kOutput, calls=%fused_computation.11 | convolution fusion | flops 4194304000 | bytes 22577152 | tf_op jit(solution)/shard_map/smc,smr->scr/dot_general | solution.py:77
  148.4 5.5 convolution_bitcast_fusion.2
  157.6 58.0 %reduce-scatter.12.cloned.1.call-done = f32[2,128,256]{1,2,0:T(8,128)} async-done(((f32[2,1024,256]{1,2,0:T(8,128)}), f32[2,128,256]{1,2,0:T(8,128)}) %reduce-scatter.12.cloned.1.call-update) | async-done | bytes 262160 | tf_op jit(solution)/shard_map/reduce_scatter | solution.py:83
  218.0 89.7 %reduce-scatter.6.cloned.1.call-done = f32[4,128,256]{1,2,0:T(8,128)} async-done(((f32[4,1024,256]{1,2,0:T(8,128)}), f32[4,128,256]{1,2,0:T(8,128)}) %reduce-scatter.6.cloned.1.call-update) | async-done | bytes 524304 | tf_op jit(solution)/shard_map/reduce_scatter | solution.py:81
  307.7 3.2 fusion.51
  310.8 89.0 %reduce-scatter.10.cloned.1.call-done = f32[4,128,256]{1,2,0:T(8,128)} async-done(((f32[4,1024,256]{1,2,0:T(8,128)}), f32[4,128,256]{1,2,0:T(8,128)}) %reduce-scatter.10.cloned.1.call-update) | async-done | bytes 524304 | tf_op jit(solution)/shard_map/reduce_scatter | solution.py:82
  403.2 141.4 %all-reduce.9.cloned.1.call-done = (f32[4,256,256]{2,1,0:T(8,128)}, f32[4,256,256]{2,1,0:T(8,128)}, f32[2,256,256]{2,1,0:T(8,128)}) async-done(((f32[4,256,256]{2,1,0:T(8,128)}, f32[4,256,256]{2,1,0:T(8,128)}, f32[2,256,256]{2,1,0:T(8,128)}), (f32[4,256,256]{2,1,0:T(8,128)}, f32[4,256,256]{2,1,0:T(8,128)}, f32[2,256,256]{2,1,0:T(8,128)})) %all-reduce.9.cloned.1.call-update) | async-done | bytes 2621456 | tf_op jit(solution)/shard_map/psum | solution.py:85
  586.4 25.7 %all-gather.6.cloned.1.call-done = bf16[4,1024,256]{2,1,0:T(8,128)(2,1)} async-done(((bf16[4,128,256]{2,1,0:T(8,128)(2,1)}), bf16[4,1024,256]{2,1,0:T(8,128)(2,1)}) %all-gather.6.cloned.1.call-update) | async-done | bytes 2097168 | tf_op jit(solution)/shard_map/all_gather | solution.py:90
  612.2 5.5 convolution_bitcast_fusion.4
  618.2 35.5 %all-gather.12.cloned.1.call-done = bf16[2,1024,256]{2,1,0:T(8,128)(2,1)} async-done(((bf16[2,128,256]{2,1,0:T(8,128)(2,1)}), bf16[2,1024,256]{2,1,0:T(8,128)(2,1)}) %all-gather.12.cloned.1.call-update) | async-done | bytes 1048592 | tf_op jit(solution)/shard_map/all_gather | solution.py:92
  653.6 13.6 %convolution_bitcast_fusion = f32[2,4000,256]{2,1,0:T(8,128)} fusion(bf16[2,4000,1024]{2,1,0:T(8,128)(2,1)} %param.26, bf16[2,1024,256]{2,1,0:T(8,128)(2,1)} %all-gather.12.cloned.1.call-done), kind=kOutput, calls=%fused_computation.2 | convolution fusion | flops 4194304000 | bytes 25624576 | tf_op jit(solution)/shard_map/smc,scr->smr/dot_general | solution.py:95
  669.5 34.9 %all-gather.10.cloned.1.call-done = bf16[4,1024,256]{2,1,0:T(8,128)(2,1)} async-done(((bf16[4,128,256]{2,1,0:T(8,128)(2,1)}), bf16[4,1024,256]{2,1,0:T(8,128)(2,1)}) %all-gather.10.cloned.1.call-update) | async-done | bytes 2097168 | tf_op jit(solution)/shard_map/all_gather | solution.py:91
  708.0 29.6 %reduce-scatter.8.cloned.1.call-done = f32[4,128,256]{1,2,0:T(8,128)} async-done(((f32[4,512,256]{1,2,0:T(8,128)}), f32[4,128,256]{1,2,0:T(8,128)}) %reduce-scatter.8.cloned.1.call-update) | async-done | bytes 524304 | tf_op jit(solution)/shard_map/reduce_scatter | solution.py:99
  739.9 71.4 %reduce-scatter.14.cloned.1.call-done = f32[2,1000,256]{2,1,0:T(8,128)} async-done(((f32[2,4000,256]{2,1,0:T(8,128)}), f32[2,1000,256]{2,1,0:T(8,128)}) %reduce-scatter.14.cloned.1.call-update) | async-done | bytes 2048016 | tf_op jit(solution)/shard_map/reduce_scatter | solution.py:101
  811.3 6.0 divide_convert_fusion
  818.6 29.0 %all-reduce.7.cloned.1.call-done = f32[4,128,256]{2,0,1:T(4,128)} async-done(((f32[4,128,256]{2,0,1:T(4,128)}), f32[4,128,256]{2,0,1:T(4,128)}) %all-reduce.7.cloned.1.call-update) | async-done | bytes 524304
  850.1 5.9 all_gather.21
  861.1 5.4 all-gather.8.cloned.1.call-done
  866.5 6.4 subtract_convert_fusion.1
  872.9 29.8 %all-gather.14.cloned.1.call-done = bf16[2,4000,256]{2,1,0:T(8,128)(2,1)} async-done(((bf16[2,1000,256]{2,1,0:T(8,128)(2,1)}), bf16[2,4000,256]{2,1,0:T(8,128)(2,1)}) %all-gather.14.cloned.1.call-update) | async-done | bytes 4096016 | tf_op jit(solution)/shard_map/all_gather | solution.py:109
  902.7 13.3 %subtract_convert_fusion = bf16[2,4000,1024]{2,1,0:T(8,128)(2,1)} fusion(bf16[2,4000,1024]{2,1,0:T(8,128)(2,1)} %param.25, bf16[2,4000,256]{2,1,0:T(8,128)(2,1)} %all-gather.14.cloned.1.call-done, bf16[2,1024,256]{2,1,0:T(8,128)(2,1)S(1)} %copy-done.20), kind=kOutput, calls=%fused_computation | convolution fusion | flops 4235264000 | bytes 37912576 | tf_op jit(solution)/shard_map/smr,scr->smc/dot_general | solution.py:113
  (126 shorter events, 70.6 us)
Async XLA Ops:
  7.2 12.5 %copy-start = (bf16[4,1024,256]{2,1,0:T(8,128)(2,1)S(1)}, bf16[4,1024,256]{2,1,0:T(8,128)(2,1)}, u32[]{:S(2)}) copy-start(bf16[4,1024,256]{2,1,0:T(8,128)(2,1)} %param.19) | copy-start | bytes 6291460
  7.2 127.1 %all-reduce.11.cloned.1.call-start = ((), (), s32[]{:S(2)}) async-start(), calls=%async_computation.17 | async-start | bytes 10813440 | tf_op jit(solution)/shard_map/psum | solution.py:71
  25.9 189.7 %reduce-scatter.12.cloned.1.call-start = ((), (), s32[]{:S(2)}) async-start(), calls=%async_computation.11 | async-start | bytes 2359296 | tf_op jit(solution)/shard_map/reduce_scatter | solution.py:83
  147.2 160.5 %reduce-scatter.6.cloned.1.call-start = ((), (), s32[]{:S(2)}) async-start(), calls=%async_computation.5 | async-start | bytes 4718592 | tf_op jit(solution)/shard_map/reduce_scatter | solution.py:81
  153.9 246.0 %reduce-scatter.10.cloned.1.call-start = ((), (), s32[]{:S(2)}) async-start(), calls=%async_computation.9 | async-start | bytes 4718592 | tf_op jit(solution)/shard_map/reduce_scatter | solution.py:82
  157.6 387.0 %all-reduce.9.cloned.1.call-start = ((), (), s32[]{:S(2)}) async-start(), calls=%async_computation.16 | async-start | bytes 5242880 | tf_op jit(solution)/shard_map/psum | solution.py:85
  403.0 209.1 %all-gather.6.cloned.1.call-start = ((), (), s32[]{:S(2)}) async-start(), calls=%async_computation.6 | async-start | bytes 2359296 | tf_op jit(solution)/shard_map/all_gather | solution.py:90
  403.1 160.8 %copy-start.10 = (f32[256,256]{1,0:T(8,128)}, f32[256,256]{1,0:T(8,128)S(1)}, u32[]{:S(2)}) copy-start(f32[256,256]{1,0:T(8,128)S(1)} %fusion.38) | copy-start | bytes 786436
  544.5 5.2 copy-start.5
  563.9 89.8 %all-gather.12.cloned.1.call-start = ((), (), s32[]{:S(2)}) async-start(), calls=%async_computation.12 | async-start | bytes 1179648 | tf_op jit(solution)/shard_map/all_gather | solution.py:92
  576.3 128.1 %all-gather.10.cloned.1.call-start = ((), (), s32[]{:S(2)}) async-start(), calls=%async_computation.10 | async-start | bytes 2359296 | tf_op jit(solution)/shard_map/all_gather | solution.py:91
  586.4 151.1 %reduce-scatter.8.cloned.1.call-start = ((), (), s32[]{:S(2)}) async-start(), calls=%async_computation.7 | async-start | bytes 2621440 | tf_op jit(solution)/shard_map/reduce_scatter | solution.py:99
  617.7 193.5 %reduce-scatter.14.cloned.1.call-start = ((), (), s32[]{:S(2)}) async-start(), calls=%async_computation.13 | async-start | bytes 10240000 | tf_op jit(solution)/shard_map/reduce_scatter | solution.py:101
  667.3 37.1 %copy-start.3 = (bf16[4,128,1024]{2,1,0:T(8,128)(2,1)S(1)}, bf16[4,128,1024]{2,1,0:T(8,128)(2,1)}, u32[]{:S(2)}) copy-start(bf16[4,128,1024]{2,1,0:T(8,128)(2,1)} %param.21) | copy-start | bytes 3145732
  667.3 180.2 %all-reduce.7.cloned.1.call-start = ((), (), s32[]{:S(2)}) async-start(), calls=%async_computation.15 | async-start | bytes 1048576
  707.9 158.6 %all-gather.8.cloned.1.call-start = ((), (), s32[]{:S(2)}) async-start(), calls=%async_computation.8 | async-start | bytes 1310720 | tf_op jit(solution)/shard_map/all_gather | solution.py:107
  739.8 77.5 %copy-start.21 = (u32[32]{0:T(128)S(1)}, u32[32]{0:T(128)}, u32[]{:S(2)}) copy-start(u32[32]{0:T(128)} %constant.11) | copy-start | bytes 388
  739.8 107.7 %copy-start.18 = (f32[4,32,256]{2,1,0:T(8,128)S(1)}, f32[4,32,256]{2,1,0:T(8,128)}, u32[]{:S(2)}) copy-start(f32[4,32,256]{2,1,0:T(8,128)} %param.22) | copy-start | bytes 393220
  739.8 107.7 %copy-start.19 = (f32[4,32,256]{2,1,0:T(8,128)S(1)}, f32[4,32,256]{2,1,0:T(8,128)}, u32[]{:S(2)}) copy-start(f32[4,32,256]{2,1,0:T(8,128)} %param.23) | copy-start | bytes 393220
  739.8 162.8 %all-gather.14.cloned.1.call-start = ((), (), s32[]{:S(2)}) async-start(), calls=%async_computation.14 | async-start | bytes 5120000 | tf_op jit(solution)/shard_map/all_gather | solution.py:109
  817.3 38.8 %copy-start.6 = (bf16[4,1024,256]{2,1,0:T(8,128)(2,1)S(1)}, bf16[4,1024,256]{2,1,0:T(8,128)(2,1)}, u32[]{:S(2)}) copy-start(bf16[4,1024,256]{2,1,0:T(8,128)(2,1)} %all-gather.10.cloned.1.call-done) | copy-start | bytes 6291460
  859.1 7.4 copy-start.13
  861.1 41.6 %copy-start.20 = (bf16[2,1024,256]{2,1,0:T(8,128)(2,1)S(1)}, bf16[2,1024,256]{2,1,0:T(8,128)(2,1)}, u32[]{:S(2)}) copy-start(bf16[2,1024,256]{2,1,0:T(8,128)(2,1)} %all-gather.12.cloned.1.call-done) | copy-start | bytes 3145732
  902.6 13.3 %copy-start.1 = (bf16[4,1024,256]{2,1,0:T(8,128)(2,1)S(1)}, bf16[4,1024,256]{2,1,0:T(8,128)(2,1)}, u32[]{:S(2)}) copy-start(bf16[4,1024,256]{2,1,0:T(8,128)(2,1)} %param.19) | copy-start | bytes 6291460
  (11 other events, 23.6 us)
Sparse Core Ops, SparseCore 0:
  26.0 108.2 all-reduce.10
  147.3 68.2 reduce-scatter.11
  220.2 87.4 reduce-scatter.5
  311.7 88.0 reduce-scatter.9
  407.6 136.8 all-reduce.8
  564.0 48.1 all-gather.5
  614.9 38.6 all-gather.11
  656.4 48.0 all-gather.9
  707.5 29.9 reduce-scatter.7
  740.8 70.4 reduce-scatter.13
  814.3 33.1 all-reduce.6
  849.6 16.8 all-gather.7
  868.7 33.9 all-gather.13
where the time goes:
time: 931 us; the launch traced here: 923 us
  waiting for transfers between devices  748 us (80%)
  matrix products  131 us (14%)
  between operations  15.2 us (2%)
  other arithmetic  12.5 us (1%)
    psum x1, waiting for transfers between devices, per_device(): lax.psum(tuple((local_gram(back) for back in backs)), ('shard', 'tensor'))  141 us
    psum x1, waiting for transfers between devices, per_device(): lax.psum(sketch_terms[0].astype(jnp.bfloat16), 'tensor').astype(jnp.float32)  108 us
    reduce_scatter x1, waiting for transfers between devices, per_device(): lax.psum_scatter(back_terms[0], 'shard', scatter_dimension=1, tiled=True)  89.7 us
    reduce_scatter x1, waiting for transfers between devices, per_device(): lax.psum_scatter(back_terms[1], 'shard', scatter_dimension=1, tiled=True)  89 us
    reduce_scatter x1, waiting for transfers between devices, per_device(): lax.psum_scatter(proj_terms[2], 'tensor', scatter_dimension=1, tiled=True)  71.4 us
    reduce_scatter x1, waiting for transfers between devices, per_device(): lax.psum_scatter(back_terms[2], 'shard', scatter_dimension=1, tiled=True)  58 us
    all_gather x1, waiting for transfers between devices, per_device(): lax.all_gather(rounded[2], 'shard', axis=1, tiled=True)  35.5 us
    all_gather x1, waiting for transfers between devices, per_device(): lax.all_gather(rounded[1], 'shard', axis=1, tiled=True)  34.9 us
  transfers between devices with their start and end apart: 13, of which 13 were waited for; matrix products, arithmetic and copies ran while one was open for 9% of the time, Pallas kernels for 0%

commit v1 on v0

--- a/solution.py
+++ b/solution.py
@@ -1,3 +1,5 @@
+import functools
+
 import jax
 import jax.numpy as jnp
 from jax import lax
@@ -41,7 +43,20 @@
     return (first_new, second_new, direction.astype(jnp.bfloat16))
 
 
+def split_rows(flat, shapes):
+    parts = []
+    offset = 0
+    for shape in shapes:
+        size = 1
+        for dim in shape:
+            size *= dim
+        parts.append(flat[..., offset:offset + size].reshape(flat.shape[:-1] + shape))
+        offset += size
+    return parts
+
+
 def per_device(
+    tensor_size,
     wide_weight,
     wide_grad,
     wide_first,
@@ -63,54 +78,48 @@
     firsts = (wide_first, narrow_first, vocab_first)
     seconds = (wide_second, narrow_second, vocab_second)
     olds = (wide_basis, narrow_basis, vocab_basis)
+    counts = [grad.shape[0] for grad in grads]
     sketch_terms = [
-        jnp.einsum("smc,scr->smr", grad, old, preferred_element_type=jnp.float32)
+        jnp.einsum("smc,scr->smr", grad, old, preferred_element_type=jnp.float32).astype(jnp.bfloat16)
         for grad, old in zip(grads, olds)
     ]
-    sketch_sum = (
-        lax.psum(sketch_terms[0].astype(jnp.bfloat16), "tensor").astype(jnp.float32),
-        lax.psum(sketch_terms[1].astype(jnp.bfloat16), "tensor").astype(jnp.float32),
-        lax.psum(sketch_terms[2].astype(jnp.bfloat16), "tensor").astype(jnp.float32),
-    )
-    sketches = [item.astype(jnp.bfloat16) for item in sketch_sum]
+    sketches = lax.psum(tuple(sketch_terms), "tensor")
     back_terms = [
         jnp.einsum("smc,smr->scr", grad, sketch, preferred_element_type=jnp.float32)
         for grad, sketch in zip(grads, sketches)
     ]
-    backs = (
-        lax.psum_scatter(back_terms[0], "shard", scatter_dimension=1, tiled=True),
-        lax.psum_scatter(back_terms[1], "shard", scatter_dimension=1, tiled=True),
-        lax.psum_scatter(back_terms[2], "shard", scatter_dimension=1, tiled=True),
-    )
-    first_grams = lax.psum(tuple((local_gram(back) for back in backs)), ("shard", "tensor"))
-    rounded = [
-        polish_small(back, gram).astype(jnp.bfloat16) for back, gram in zip(backs, first_grams)
-    ]
-    bases = (
-        lax.all_gather(rounded[0], "shard", axis=1, tiled=True),
-        lax.all_gather(rounded[1], "shard", axis=1, tiled=True),
-        lax.all_gather(rounded[2], "shard", axis=1, tiled=True),
-    )
-    proj_terms = [
-        jnp.einsum("smc,scr->smr", grad, basis, preferred_element_type=jnp.float32)
-        for grad, basis in zip(grads, bases)
-    ]
-    projected = (
-        lax.psum_scatter(proj_terms[0], "tensor", scatter_dimension=1, tiled=True),
-        lax.psum_scatter(proj_terms[1], "tensor", scatter_dimension=1, tiled=True),
-        lax.psum_scatter(proj_terms[2], "tensor", scatter_dimension=1, tiled=True),
-    )
+    back_all = jnp.concatenate(back_terms, axis=0).astype(jnp.bfloat16)
+    backs = lax.psum_scatter(back_all, "shard", scatter_dimension=1, tiled=True).astype(jnp.float32)
+    grams = lax.psum(local_gram(backs), ("shard", "tensor"))
+    rounded = polish_small(backs, grams).astype(jnp.bfloat16)
+    basis_all = lax.all_gather(rounded, "shard", axis=1, tiled=True)
+    bases = []
+    offset = 0
+    for count in counts:
+        bases.append(basis_all[offset:offset + count])
+        offset += count
+    proj_parts = []
+    row_shapes = []
+    for grad, basis in zip(grads, bases):
+        count, rows, cols = grad.shape
+        split = grad.reshape(count, tensor_size, rows // tensor_size, cols)
+        proj = jnp.einsum("sjmc,scr->jsmr", split, basis, preferred_element_type=jnp.float32)
+        row_shapes.append((count, rows // tensor_size, basis.shape[2]))
+        proj_parts.append(proj.reshape(tensor_size, -1, basis.shape[2]).astype(jnp.bfloat16))
+    proj_all = jnp.concatenate(proj_parts, axis=1)
+    proj_mine = lax.psum_scatter(proj_all, "tensor", scatter_dimension=0, tiled=True).reshape(-1)
+    projected = [part.astype(jnp.float32) for part in split_rows(proj_mine, row_shapes)]
     results = [
         adam_moments(first, second, proj) for first, second, proj in zip(firsts, seconds, projected)
     ]
-    directions = (
-        lax.all_gather(results[0][2], "tensor", axis=1, tiled=True),
-        lax.all_gather(results[1][2], "tensor", axis=1, tiled=True),
-        lax.all_gather(results[2][2], "tensor", axis=1, tiled=True),
-    )
+    dir_all = jnp.concatenate([result[2].reshape(-1) for result in results])
+    dir_gathered = lax.all_gather(dir_all, "tensor", axis=0, tiled=False)
+    directions = split_rows(dir_gathered, row_shapes)
     outputs = []
     for weight, direction, basis, result in zip(weights, directions, bases, results):
-        update = jnp.einsum("smr,scr->smc", direction, basis, preferred_element_type=jnp.float32)
+        count, rows, cols = weight.shape
+        update = jnp.einsum("jsmr,scr->sjmc", direction, basis, preferred_element_type=jnp.float32)
+        update = update.reshape(count, rows, cols)
         weight_new = (0.99 * weight.astype(jnp.float32) - 2.0 * update).astype(jnp.bfloat16)
         outputs.append((weight_new, result[0], result[1]))
     return (
@@ -156,5 +165,5 @@
         P(None, ("shard", "tensor"), None),
     )
     return jax.shard_map(
-        per_device, mesh=mesh, in_specs=in_specs, out_specs=out_specs, check_vma=False
+        functools.partial(per_device, mesh.shape["tensor"]), mesh=mesh, in_specs=in_specs, out_specs=out_specs, check_vma=False
     )

time: 931 us -> 737 us (0.79)
  waiting for transfers between devices: 748 us -> 526 us
  other arithmetic: 12.5 us -> 45.9 us
  local copies, waits for them, and re-layouts: 8.78 us -> 40.7 us
  matrix products: 131 us -> 103 us
    reduce_scatter x5 -> x1, waiting for transfers between devices: 338 us -> 50.4 us  [per_device(): lax.psum_scatter(proj_all, 'tensor', scatter_dimension=0, tiled=True)]
    unnamed x14 -> x7, waiting for transfers between devices: 29.2 us -> 103 us
    convert_element_type x0 -> x3, other arithmetic: none -> 31.1 us  [per_device(): (0.99 * weight.astype(jnp.float32) - 2.0 * update).astype(jnp.bfloat16)]
    unnamed x51 -> x48, local copies, waits for them, and re-layouts: 7.78 us -> 28.2 us
    dot_general x6, matrix products: 44.4 us -> 33.1 us  [the longest x3 19.8 us: per_device(): jnp.einsum('jsmr,scr->sjmc', direction, basis, preferred_element_type=jnp...]
    all_gather x5 -> x2, waiting for transfers between devices: 131 us -> 126 us  [the longest x1 84.8 us: per_device(): basis_all = lax.all_gather(rounded, 'shard', axis=1, tiled=True)]
  transfers between devices with their start and end apart: 13 -> 6, of which waited for: 13 -> 6; matrix products, arithmetic and copies ran while one was open for 9% -> 0% of each run, Pallas kernels for 0% -> 0%
where the time goes in v1:
time: 737 us; the launch traced here: 732 us
  waiting for transfers between devices  526 us (71%)
  matrix products  103 us (14%)
  other arithmetic  45.9 us (6%)
  local copies, waits for them, and re-layouts  40.7 us (6%)
  between operations  14.7 us (2%)
    psum x1, waiting for transfers between devices, per_device(): grams = lax.psum(local_gram(backs), ('shard', 'tensor'))  138 us
    psum x1, waiting for transfers between devices, per_device(): sketches = lax.psum(tuple(sketch_terms), 'tensor')  108 us
    unnamed x7, waiting for transfers between devices  103 us
    all_gather x1, waiting for transfers between devices, per_device(): basis_all = lax.all_gather(rounded, 'shard', axis=1, tiled=True)  84.8 us
    reduce_scatter x1, waiting for transfers between devices, per_device(): lax.psum_scatter(proj_all, 'tensor', scatter_dimension=0, tiled=True)  50.4 us
    all_gather x1, waiting for transfers between devices, per_device(): dir_gathered = lax.all_gather(dir_all, 'tensor', axis=0, tiled=False)  41.5 us
    convert_element_type x3, other arithmetic, per_device(): (0.99 * weight.astype(jnp.float32) - 2.0 * update).astype(jnp.bfloat16)  31.1 us
    unnamed x48, local copies, waits for them, and re-layouts  28.2 us
  transfers between devices with their start and end apart: 6, of which 6 were waited for; matrix products, arithmetic and copies ran while one was open for 0% of the time, Pallas kernels for 0%

profile of v1, /device:TPU:0, one launch (start us, length us, event | category | flops | bytes accessed | tf_op | source)
XLA Modules:
  0.0 731.9 jit_solution(9271300986264332978)
XLA Ops:
  10.4 4.5 convolution_convert_fusion.2
  14.9 12.1 %convolution_convert_fusion = bf16[2,4000,256]{2,1,0:T(8,128)(2,1)} fusion(bf16[2,4000,1024]{2,1,0:T(8,128)(2,1)} %param.26, bf16[2,1024,256]{2,1,0:T(8,128)(2,1)S(1)} %copy-done.16), kind=kOutput, calls=%fused_computation.5 | convolution fusion | flops 4196352000 | bytes 21528576 | tf_op jit(solution)/shard_map/smc,scr->smr/dot_general | solution.py:83
  27.4 108.1 %all-reduce.6.cloned.1.call-done = (bf16[2,4000,256]{2,1,0:T(8,128)(2,1)}, bf16[4,128,256]{2,1,0:T(8,128)(2,1)}, bf16[4,512,256]{2,1,0:T(8,128)(2,1)}) async-done(((bf16[2,4000,256]{2,1,0:T(8,128)(2,1)}, bf16[4,128,256]{2,1,0:T(8,128)(2,1)}, bf16[4,512,256]{2,1,0:T(8,128)(2,1)}), (bf16[2,4000,256]{2,1,0:T(8,128)(2,1)}, bf16[4,128,256]{2,1,0:T(8,128)(2,1)}, ...) | async-done | bytes 5406736 | tf_op jit(solution)/shard_map/psum | solution.py:86
  135.5 11.6 %fusion.32 = bf16[2,1024,256]{1,2,0:T(8,128)(2,1)S(1)} fusion(bf16[2,4000,256]{2,1,0:T(8,128)(2,1)} %get-tuple-element.9, bf16[2,4000,1024]{2,1,0:T(8,128)(2,1)} %param.26), kind=kOutput, calls=%fused_computation.55 | convolution fusion | flops 4194828288 | bytes 21528576 | tf_op jit(solution)/shard_map/smc,smr->scr/dot_general | solution.py:88
  152.5 11.6 %copy.51 = bf16[10,1024,256]{2,0,1:T(8,128)(2,1)} copy(bf16[10,1024,256]{1,2,0:T(8,128)(2,1)} %pad_maximum_fusion.1) | data formatting | bytes 10485760
  164.1 9.2 %copy.53 = bf16[128,8,10,256]{3,1,2,0:T(8,128)(2,1)} copy(bf16[128,8,10,256]{3,2,1,0:T(8,128)(2,1)} %bitcast.110) | data formatting | bytes 10485760
  173.4 103.0 %reduce-scatter.7.cloned.1.call-done = bf16[128,2560]{1,0:T(8,128)(2,1)} async-done(((bf16[1024,2560]{1,0:T(8,128)(2,1)}), bf16[128,2560]{1,0:T(8,128)(2,1)}) %reduce-scatter.7.cloned.1.call-update) | async-done | bytes 655376
  281.4 137.8 %all-reduce.4.cloned.1.call-done = f32[10,256,256]{2,1,0:T(8,128)} async-done(((f32[10,256,256]{2,1,0:T(8,128)}), f32[10,256,256]{2,1,0:T(8,128)}) %all-reduce.4.cloned.1.call-update) | async-done | bytes 2621456 | tf_op jit(solution)/shard_map/psum | solution.py:93
  424.9 3.5 fusion.15
  428.3 3.3 fusion.14
  434.8 3.3 fusion.9
  440.8 3.3 fusion.10
  444.1 3.5 fusion.8
  453.5 3.3 convolution_convert_fusion.3
  456.8 84.8 %all-gather.4.cloned.1.call-done = bf16[10,1024,256]{2,1,0:T(8,128)(2,1)} async-done(((bf16[10,128,256]{2,1,0:T(8,128)(2,1)}), bf16[10,1024,256]{2,1,0:T(8,128)(2,1)}) %all-gather.4.cloned.1.call-update) | async-done | bytes 5242896 | tf_op jit(solution)/shard_map/all_gather | solution.py:95
  547.4 8.3 %convert_bitcast_fusion = bf16[4,2,1000,256]{3,2,0,1:T(8,128)(2,1)S(1)} fusion(bf16[2,4,1000,1024]{3,2,1,0:T(8,128)(2,1)} %bitcast.134, bf16[10,1024,256]{2,1,0:T(8,128)(2,1)} %all-gather.4.cloned.1.call-done), kind=kOutput, calls=%fused_computation.10 | convolution fusion | flops 4196352000 | bytes 21528576 | tf_op jit(solution)/shard_map/sjmc,scr->jsmr/dot_general | solution.py:106
  559.3 50.4 %reduce-scatter.5.cloned.1.call-done = bf16[1,2640,256]{2,1,0:T(8,128)(2,1)} async-done(((bf16[4,2640,256]{2,1,0:T(8,128)(2,1)}), bf16[1,2640,256]{2,1,0:T(8,128)(2,1)}) %reduce-scatter.5.cloned.1.call-update) | async-done | bytes 1351696 | tf_op jit(solution)/shard_map/reduce_scatter | solution.py:110
  615.2 3.5 divide_convert_fusion
  621.0 41.5 %all-gather.6.cloned.1.call-done = bf16[2703360]{0:T(1024)(128)(2,1)} async-done(((bf16[675840]{0:T(1024)(128)(2,1)}), bf16[2703360]{0:T(1024)(128)(2,1)}) %all-gather.6.cloned.1.call-update) | async-done | bytes 5406736 | tf_op jit(solution)/shard_map/all_gather | solution.py:116
  662.5 6.9 reshape.109
  676.2 4.7 broadcast_multiply_fusion
  680.9 7.2 fusion.1
  688.1 14.3 %convolution_multiply_fusion = f32[2,4,1000,1024]{3,2,1,0:T(8,128)} fusion(bf16[4,2,1000,256]{3,2,1,0:T(8,128)(2,1)S(1)} %bitcast.109, bf16[10,1024,256]{2,1,0:T(8,128)(2,1)} %all-gather.4.cloned.1.call-done), kind=kOutput, calls=%fused_computation.2 | convolution fusion | flops 4202496000 | bytes 37912576 | tf_op jit(solution)/shard_map/jsmr,scr->sjmc/dot_general | solution.py:121
  702.3 22.5 %fusion = bf16[2,4000,1024]{2,1,0:T(8,128)(2,1)} fusion(f32[2,4,1000,1024]{3,2,1,0:T(8,128)} %convolution_multiply_fusion, bf16[2,4000,1024]{2,1,0:T(8,128)(2,1)} %param.25), kind=kLoop, calls=%fused_computation.1 | loop fusion | flops 32768000 | bytes 65536000 | tf_op jit(solution)/shard_map/convert_element_type | solution.py:123
  (95 shorter events, 55.2 us)
Async XLA Ops:
  7.2 3.3 copy-start
  7.2 128.3 %all-reduce.6.cloned.1.call-start = ((), (), s32[]{:S(2)}) async-start(), calls=%async_computation.7 | async-start | bytes 10813440 | tf_op jit(solution)/shard_map/psum | solution.py:86
  10.4 4.5 copy-start.16
  27.0 249.4 %reduce-scatter.7.cloned.1.call-start = ((), (), s32[]{:S(2)}) async-start(), calls=%async_computation.6 | async-start | bytes 5898240
  135.5 11.6 %copy-start.5 = (bf16[4,128,1024]{2,1,0:T(8,128)(2,1)S(1)}, bf16[4,128,1024]{2,1,0:T(8,128)(2,1)}, u32[]{:S(2)}) copy-start(bf16[4,128,1024]{2,1,0:T(8,128)(2,1)} %param.21) | copy-start | bytes 3145732
  135.5 11.6 %copy-start.13 = (bf16[4,128,256]{2,1,0:T(8,128)(2,1)S(1)}, bf16[4,128,256]{2,1,0:T(8,128)(2,1)}, u32[]{:S(2)}) copy-start(bf16[4,128,256]{2,1,0:T(8,128)(2,1)} %get-tuple-element.10) | copy-start | bytes 786436
  135.5 12.4 %copy-start.3 = (bf16[4,512,1024]{2,1,0:T(8,128)(2,1)S(1)}, bf16[4,512,1024]{2,1,0:T(8,128)(2,1)}, u32[]{:S(2)}) copy-start(bf16[4,512,1024]{2,1,0:T(8,128)(2,1)} %param.16) | copy-start | bytes 12582916
  173.4 245.9 %all-reduce.4.cloned.1.call-start = ((), (), s32[]{:S(2)}) async-start(), calls=%async_computation.2 | async-start | bytes 5242880 | tf_op jit(solution)/shard_map/psum | solution.py:93
  280.8 260.9 %all-gather.4.cloned.1.call-start = ((), (), s32[]{:S(2)}) async-start(), calls=%async_computation.3 | async-start | bytes 5898240 | tf_op jit(solution)/shard_map/all_gather | solution.py:95
  419.3 2.5 copy-start.2
  456.8 152.9 %reduce-scatter.5.cloned.1.call-start = ((), (), s32[]{:S(2)}) async-start(), calls=%async_computation.4 | async-start | bytes 6758400 | tf_op jit(solution)/shard_map/reduce_scatter | solution.py:110
  541.7 2.8 copy-start.4
  558.8 51.7 %copy-start.14 = (f32[4,32,256]{2,1,0:T(8,128)S(1)}, f32[4,32,256]{2,1,0:T(8,128)}, u32[]{:S(2)}) copy-start(f32[4,32,256]{2,1,0:T(8,128)} %param.22) | copy-start | bytes 393220
  558.8 51.7 %copy-start.15 = (f32[4,32,256]{2,1,0:T(8,128)S(1)}, f32[4,32,256]{2,1,0:T(8,128)}, u32[]{:S(2)}) copy-start(f32[4,32,256]{2,1,0:T(8,128)} %param.23) | copy-start | bytes 393220
  558.8 53.5 %copy-start.11 = (f32[4,128,256]{2,1,0:T(8,128)S(1)}, f32[4,128,256]{2,1,0:T(8,128)}, u32[]{:S(2)}) copy-start(f32[4,128,256]{2,1,0:T(8,128)} %param.17) | copy-start | bytes 1572868
  558.8 53.5 %copy-start.12 = (f32[4,128,256]{2,1,0:T(8,128)S(1)}, f32[4,128,256]{2,1,0:T(8,128)}, u32[]{:S(2)}) copy-start(f32[4,128,256]{2,1,0:T(8,128)} %param.18) | copy-start | bytes 1572868
  558.9 103.6 %all-gather.6.cloned.1.call-start = ((), (), s32[]{:S(2)}) async-start(), calls=%async_computation.5 | async-start | bytes 6758400 | tf_op jit(solution)/shard_map/all_gather | solution.py:116
  612.3 2.3 copy-start.8
  612.3 2.9 copy-start.9
  669.4 2.3 slice-start.2
  669.4 4.1 slice-start.3
  671.7 2.0 slice-start.4
  676.2 4.7 copy-start.6
  702.3 22.5 %copy-start.1 = (bf16[4,1024,256]{2,1,0:T(8,128)(2,1)S(1)}, bf16[4,1024,256]{2,1,0:T(8,128)(2,1)}, u32[]{:S(2)}) copy-start(bf16[4,1024,256]{2,1,0:T(8,128)(2,1)} %param.19) | copy-start | bytes 6291460
  (5 other events, 6.7 us)
Sparse Core Ops, SparseCore 0:
  27.2 108.2 all-reduce.5
  173.5 102.8 reduce-scatter.6
  283.3 135.8 all-reduce.3
  456.9 84.6 all-gather.3
  559.0 50.6 reduce-scatter.4
  621.1 41.3 all-gather.5

commit v2 on v1

--- a/solution.py
+++ b/solution.py
@@ -89,10 +89,9 @@
         for grad, sketch in zip(grads, sketches)
     ]
     back_all = jnp.concatenate(back_terms, axis=0).astype(jnp.bfloat16)
-    backs = lax.psum_scatter(back_all, "shard", scatter_dimension=1, tiled=True).astype(jnp.float32)
-    grams = lax.psum(local_gram(backs), ("shard", "tensor"))
-    rounded = polish_small(backs, grams).astype(jnp.bfloat16)
-    basis_all = lax.all_gather(rounded, "shard", axis=1, tiled=True)
+    backs = lax.psum(back_all, "shard").astype(jnp.float32)
+    grams = lax.psum(local_gram(backs), "tensor")
+    basis_all = polish_small(backs, grams).astype(jnp.bfloat16)
     bases = []
     offset = 0
     for count in counts:

time: 737 us -> 654 us (0.89)
  waiting for transfers between devices: 526 us -> 445 us
  local copies, waits for them, and re-layouts: 40.7 us -> 22.2 us
  matrix products: 103 us -> 120 us
    psum x1 -> x2, waiting for transfers between devices: 138 us -> 243 us  [the longest x1 184 us: per_device(): backs = lax.psum(back_all, 'shard').astype(jnp.float32)]
    unnamed x7 -> x5, waiting for transfers between devices: 103 us -> 0.08 us
    all_gather x1 -> x0, waiting for transfers between devices: 84.8 us -> none  [per_device(): basis_all = lax.all_gather(rounded, 'shard', axis=1, tiled=True)]
    unnamed x48 -> x52, local copies, waits for them, and re-layouts: 28.2 us -> 9 us
    dot_general x1, matrix products: 3.29 us -> 17.6 us  [polish_small(): jnp.einsum('sdk,skl->sdl', back * scale[:, None, None], factor, precision...]
  transfers between devices with their start and end apart: 6 -> 5, of which waited for: 6 -> 5; matrix products, arithmetic and copies ran while one was open for 0% -> 0% of each run, Pallas kernels for 0% -> 0%
where the time goes in v2:
time: 654 us; the launch traced here: 649 us
  waiting for transfers between devices  445 us (68%)
  matrix products  120 us (18%)
  other arithmetic  45.9 us (7%)
  local copies, waits for them, and re-layouts  22.2 us (3%)
  between operations  14.7 us (2%)
    psum x1, waiting for transfers between devices, per_device(): backs = lax.psum(back_all, 'shard').astype(jnp.float32)  184 us
    psum x1, waiting for transfers between devices, per_device(): sketches = lax.psum(tuple(sketch_terms), 'tensor')  108 us
    psum x1, waiting for transfers between devices, per_device(): grams = lax.psum(local_gram(backs), 'tensor')  58.7 us
    reduce_scatter x1, waiting for transfers between devices, per_device(): lax.psum_scatter(proj_all, 'tensor', scatter_dimension=0, tiled=True)  52.7 us
    all_gather x1, waiting for transfers between devices, per_device(): dir_gathered = lax.all_gather(dir_all, 'tensor', axis=0, tiled=False)  41.5 us
    convert_element_type x3, other arithmetic, per_device(): (0.99 * weight.astype(jnp.float32) - 2.0 * update).astype(jnp.bfloat16)  31.1 us
    dot_general x3, matrix products, per_device(): jnp.einsum('jsmr,scr->sjmc', direction, basis, preferred_element_type=jnp...  19.9 us
    dot_general x3, matrix products, per_device(): jnp.einsum('smc,scr->smr', grad, old, preferred_element_type=jnp.float32)  19.8 us
  transfers between devices with their start and end apart: 5, of which 5 were waited for; matrix products, arithmetic and copies ran while one was open for 0% of the time, Pallas kernels for 0%

profile of v2, /device:TPU:0, one launch (start us, length us, event | category | flops | bytes accessed | tf_op | source)
XLA Modules:
  0.0 648.6 jit_solution(3402719236633142392)
XLA Ops:
  7.2 3.2 convolution_convert_fusion.3
  10.4 4.5 convolution_convert_fusion.2
  14.9 12.1 %convolution_convert_fusion = bf16[2,4000,256]{2,1,0:T(8,128)(2,1)} fusion(bf16[2,4000,1024]{2,1,0:T(8,128)(2,1)} %param.26, bf16[2,1024,256]{2,1,0:T(8,128)(2,1)S(1)} %copy-done.18), kind=kOutput, calls=%fused_computation.8 | convolution fusion | flops 4196352000 | bytes 21528576 | tf_op jit(solution)/shard_map/smc,scr->smr/dot_general | solution.py:83
  27.3 108.2 %all-reduce.9.cloned.1.call-done = (bf16[2,4000,256]{2,1,0:T(8,128)(2,1)}, bf16[4,128,256]{2,1,0:T(8,128)(2,1)}, bf16[4,512,256]{2,1,0:T(8,128)(2,1)}) async-done(((bf16[2,4000,256]{2,1,0:T(8,128)(2,1)}, bf16[4,128,256]{2,1,0:T(8,128)(2,1)}, bf16[4,512,256]{2,1,0:T(8,128)(2,1)}), (bf16[2,4000,256]{2,1,0:T(8,128)(2,1)}, bf16[4,128,256]{2,1,0:T(8,128)(2,1)}, ...) | async-done | bytes 5406736 | tf_op jit(solution)/shard_map/psum | solution.py:86
  135.5 11.6 %fusion.39 = bf16[2,1024,256]{1,2,0:T(8,128)(2,1)S(1)} fusion(bf16[2,4000,256]{2,1,0:T(8,128)(2,1)} %get-tuple-element.9, bf16[2,4000,1024]{2,1,0:T(8,128)(2,1)} %param.26), kind=kOutput, calls=%fused_computation.60 | convolution fusion | flops 4194828288 | bytes 21528576 | tf_op jit(solution)/shard_map/smc,smr->scr/dot_general | solution.py:88
  152.6 184.3 %all-reduce.5.cloned.1.call-done = bf16[10,1024,256]{1,2,0:T(8,128)(2,1)} async-done(((bf16[10,1024,256]{1,2,0:T(8,128)(2,1)}), bf16[10,1024,256]{1,2,0:T(8,128)(2,1)}) %all-reduce.5.cloned.1.call-update) | async-done | bytes 5242896 | tf_op jit(solution)/shard_map/psum | solution.py:92
  336.9 7.1 %fusion.97 = f32[10,256,256]{2,1,0:T(8,128)} fusion(bf16[10,1024,256]{1,2,0:T(8,128)(2,1)} %all-reduce.5.cloned.1.call-done), kind=kOutput, calls=%fused_computation.126 | convolution fusion | flops 1342177280 | bytes 7864320 | tf_op jit(solution)/shard_map/sdk,sdl->skl/dot_general | solution.py:15
  344.3 58.7 %all-reduce.7.cloned.1.call-done = f32[10,256,256]{2,1,0:T(8,128)} async-done(((f32[10,256,256]{2,1,0:T(8,128)}), f32[10,256,256]{2,1,0:T(8,128)}) %all-reduce.7.cloned.1.call-update) | async-done | bytes 2621456 | tf_op jit(solution)/shard_map/psum | solution.py:93
  408.6 3.5 fusion.22
  412.1 3.3 fusion.21
  415.4 3.3 fusion.98
  418.8 3.3 fusion.16
  424.8 3.3 fusion.17
  428.1 3.4 fusion.15
  437.4 17.6 %fusion.7 = bf16[10,1024,256]{2,1,0:T(8,128)(2,1)S(1)} fusion(f32[10,256,256]{2,1,0:T(8,128)S(1)} %fusion.10, bf16[10,1024,256]{1,2,0:T(8,128)(2,1)S(1)} %bitcast.105, f32[10]{0:T(128)S(1)} %get-tuple-element.21), kind=kOutput, calls=%fused_computation.18 | convolution fusion | flops 8060928000 | bytes 13107240 | tf_op jit(solution)/shard_map/sdk,skl->sdl/dot_general | solution.py:36
  460.7 8.2 %convert_bitcast_fusion = bf16[4,2,1000,256]{3,2,0,1:T(8,128)(2,1)S(1)} fusion(bf16[2,4,1000,1024]{3,2,1,0:T(8,128)(2,1)} %bitcast.128, bf16[10,1024,256]{2,1,0:T(8,128)(2,1)S(1)} %fusion.7), kind=kOutput, calls=%fused_computation.14 | convolution fusion | flops 4196352000 | bytes 21528576 | tf_op jit(solution)/shard_map/sjmc,scr->jsmr/dot_general | solution.py:105
  472.7 52.7 %reduce-scatter.2.cloned.1.call-done = bf16[1,2640,256]{2,1,0:T(8,128)(2,1)} async-done(((bf16[4,2640,256]{2,1,0:T(8,128)(2,1)}), bf16[1,2640,256]{2,1,0:T(8,128)(2,1)}) %reduce-scatter.2.cloned.1.call-update) | async-done | bytes 1351696 | tf_op jit(solution)/shard_map/reduce_scatter | solution.py:109
  530.9 3.5 divide_convert_fusion
  536.7 41.5 %all-gather.3.cloned.1.call-done = bf16[2703360]{0:T(1024)(128)(2,1)} async-done(((bf16[675840]{0:T(1024)(128)(2,1)}), bf16[2703360]{0:T(1024)(128)(2,1)}) %all-gather.3.cloned.1.call-update) | async-done | bytes 5406736 | tf_op jit(solution)/shard_map/all_gather | solution.py:115
  578.2 6.9 %reshape.109 = bf16[4,675840]{1,0:T(4,128)(2,1)} reshape(bf16[2703360]{0:T(1024)(128)(2,1)} %all-gather.3.cloned.1.call-done) | data formatting | bytes 10813440 | tf_op jit(solution)/shard_map/all_gather | solution.py:115
  590.2 4.7 broadcast_multiply_fusion
  594.9 14.4 %convolution_multiply_fusion = f32[2,4,1000,1024]{3,2,1,0:T(8,128)} fusion(bf16[4,2,1000,256]{3,2,1,0:T(8,128)(2,1)S(1)} %bitcast.106, bf16[10,1024,256]{2,1,0:T(8,128)(2,1)} %copy-done.3), kind=kOutput, calls=%fused_computation.2 | convolution fusion | flops 4202496000 | bytes 37912576 | tf_op jit(solution)/shard_map/jsmr,scr->sjmc/dot_general | solution.py:120
  611.9 7.2 %fusion.4 = bf16[4,512,1024]{2,1,0:T(8,128)(2,1)} fusion(f32[4,4,128,1024]{3,2,1,0:T(8,128)} %broadcast_multiply_fusion, bf16[4,512,1024]{2,1,0:T(8,128)(2,1)S(1)} %copy-done.7), kind=kLoop, calls=%fused_computation.7 | loop fusion | flops 8388608 | bytes 16777216 | tf_op jit(solution)/shard_map/convert_element_type | solution.py:122
  619.1 22.5 %fusion = bf16[2,4000,1024]{2,1,0:T(8,128)(2,1)} fusion(f32[2,4,1000,1024]{3,2,1,0:T(8,128)} %convolution_multiply_fusion, bf16[2,4000,1024]{2,1,0:T(8,128)(2,1)} %param.25), kind=kLoop, calls=%fused_computation.1 | loop fusion | flops 32768000 | bytes 65536000 | tf_op jit(solution)/shard_map/convert_element_type | solution.py:122
  (97 shorter events, 44.9 us)
Async XLA Ops:
  7.2 3.3 copy-start
  7.2 128.3 %all-reduce.9.cloned.1.call-start = ((), (), s32[]{:S(2)}) async-start(), calls=%async_computation.5 | async-start | bytes 10813440 | tf_op jit(solution)/shard_map/psum | solution.py:86
  10.4 4.5 copy-start.18
  27.0 309.8 %all-reduce.5.cloned.1.call-start = ((), (), s32[]{:S(2)}) async-start(), calls=%async_computation.1 | async-start | bytes 10485760 | tf_op jit(solution)/shard_map/psum | solution.py:92
  135.5 11.6 %copy-start.6 = (bf16[4,128,1024]{2,1,0:T(8,128)(2,1)S(1)}, bf16[4,128,1024]{2,1,0:T(8,128)(2,1)}, u32[]{:S(2)}) copy-start(bf16[4,128,1024]{2,1,0:T(8,128)(2,1)} %param.21) | copy-start | bytes 3145732
  135.5 11.6 %copy-start.15 = (bf16[4,128,256]{2,1,0:T(8,128)(2,1)S(1)}, bf16[4,128,256]{2,1,0:T(8,128)(2,1)}, u32[]{:S(2)}) copy-start(bf16[4,128,256]{2,1,0:T(8,128)(2,1)} %get-tuple-element.10) | copy-start | bytes 786436
  135.5 12.4 %copy-start.4 = (bf16[4,512,1024]{2,1,0:T(8,128)(2,1)S(1)}, bf16[4,512,1024]{2,1,0:T(8,128)(2,1)}, u32[]{:S(2)}) copy-start(bf16[4,512,1024]{2,1,0:T(8,128)(2,1)} %param.16) | copy-start | bytes 12582916
  152.5 250.5 %all-reduce.7.cloned.1.call-start = ((), (), s32[]{:S(2)}) async-start(), calls=%async_computation.2 | async-start | bytes 5242880 | tf_op jit(solution)/shard_map/psum | solution.py:93
  344.0 181.4 %reduce-scatter.2.cloned.1.call-start = ((), (), s32[]{:S(2)}) async-start(), calls=%async_computation.3 | async-start | bytes 6758400 | tf_op jit(solution)/shard_map/reduce_scatter | solution.py:109
  403.0 2.5 copy-start.2
  431.5 5.9 slice-start
  434.2 3.2 slice-start.1
  455.1 5.6 copy-start.3
  455.1 4.2 copy-start.5
  472.6 53.6 %copy-start.16 = (f32[4,32,256]{2,1,0:T(8,128)S(1)}, f32[4,32,256]{2,1,0:T(8,128)}, u32[]{:S(2)}) copy-start(f32[4,32,256]{2,1,0:T(8,128)} %param.22) | copy-start | bytes 393220
  472.6 53.6 %copy-start.17 = (f32[4,32,256]{2,1,0:T(8,128)S(1)}, f32[4,32,256]{2,1,0:T(8,128)}, u32[]{:S(2)}) copy-start(f32[4,32,256]{2,1,0:T(8,128)} %param.23) | copy-start | bytes 393220
  472.6 55.4 %copy-start.13 = (f32[4,128,256]{2,1,0:T(8,128)S(1)}, f32[4,128,256]{2,1,0:T(8,128)}, u32[]{:S(2)}) copy-start(f32[4,128,256]{2,1,0:T(8,128)} %param.17) | copy-start | bytes 1572868
  472.6 55.4 %copy-start.14 = (f32[4,128,256]{2,1,0:T(8,128)S(1)}, f32[4,128,256]{2,1,0:T(8,128)}, u32[]{:S(2)}) copy-start(f32[4,128,256]{2,1,0:T(8,128)} %param.18) | copy-start | bytes 1572868
  472.7 105.5 %all-gather.3.cloned.1.call-start = ((), (), s32[]{:S(2)}) async-start(), calls=%async_computation.4 | async-start | bytes 6758400 | tf_op jit(solution)/shard_map/all_gather | solution.py:115
  528.0 2.9 copy-start.10
  585.1 4.1 slice-start.5
  594.9 14.4 %copy-start.11 = (bf16[4,128,1024]{2,1,0:T(8,128)(2,1)S(1)}, bf16[4,128,1024]{2,1,0:T(8,128)(2,1)}, u32[]{:S(2)}) copy-start(bf16[4,128,1024]{2,1,0:T(8,128)(2,1)} %param.20) | copy-start | bytes 3145732
  609.3 2.6 copy-start.7
  619.1 22.5 %copy-start.1 = (bf16[4,1024,256]{2,1,0:T(8,128)(2,1)S(1)}, bf16[4,1024,256]{2,1,0:T(8,128)(2,1)}, u32[]{:S(2)}) copy-start(bf16[4,1024,256]{2,1,0:T(8,128)(2,1)} %param.19) | copy-start | bytes 6291460
  (8 other events, 12.9 us)
Sparse Core Ops, SparseCore 0:
  27.2 108.2 all-reduce.8
  152.6 184.1 all-reduce.4
  344.1 58.8 all-reduce.6
  472.8 52.5 reduce-scatter.1
  536.8 41.3 all-gather.2

commit v3 on v2

v3 whole, which is shorter than its diff:
```python
import functools

import jax
import jax.numpy as jnp
from jax import lax
from jax.experimental import pallas as pl
from jax.sharding import PartitionSpec as P

NS_ITERS = 3


HIGHEST = lax.Precision.HIGHEST
HIGH = lax.Precision.HIGH


def local_gram(back):
    return jnp.einsum("sdk,sdl->skl", back, back, preferred_element_type=jnp.float32)


def symmetric_psum(gram, axis):
    half = gram.shape[1] // 2
    top, corner = lax.psum((gram[:, :half, :], gram[:, half:, half:]), axis)
    bottom = jnp.concatenate([jnp.swapaxes(top[:, :, half:], 1, 2), corner], axis=2)
    return jnp.concatenate([top, bottom], axis=1)


def polish_small(back, gram):
    trace = jnp.einsum("skk->s", gram)
    scale = 1.0 / jnp.sqrt(trace + 1e-06)
    small = gram * (scale * scale)[:, None, None]
    rank = gram.shape[1]
    eye = jnp.eye(rank, dtype=jnp.float32)[None, :, :]
    factor = None
    for step in range(NS_ITERS):
        square = jnp.einsum("skl,slm->skm", small, small, precision=HIGH)
        turn = 3.4445 * eye - 4.775 * small + 2.0315 * square
        if factor is None:
            factor = turn
        else:
            factor = jnp.einsum("skl,slm->skm", factor, turn, precision=HIGH)
        if step + 1 < NS_ITERS:
            small = jnp.einsum(
                "skl,slm->skm",
                turn,
                jnp.einsum("skl,slm->skm", small, turn, precision=HIGH),
                precision=HIGH,
            )
    return apply_polish(back, factor, scale)


def polish_kernel(back_ref, factor_ref, scale_ref, out_ref):
    back = back_ref[0]
    factor = factor_ref[0]
    high = factor.astype(jnp.bfloat16)
    low = (factor - high.astype(jnp.float32)).astype(jnp.bfloat16)
    polished = jnp.dot(back, high, preferred_element_type=jnp.float32)
    polished = polished + jnp.dot(back, low, preferred_element_type=jnp.float32)
    out_ref[0] = (polished * scale_ref[0, 0:1, 0:1]).astype(out_ref.dtype)


def apply_polish(back, factor, scale):
    count, rows, rank = back.shape
    scales = jnp.broadcast_to(scale[:, None, None], (count, 8, 128))
    return pl.pallas_call(
        polish_kernel,
        grid=(count,),
        in_specs=[
            pl.BlockSpec((1, rows, rank), lambda s: (s, 0, 0)),
            pl.BlockSpec((1, rank, rank), lambda s: (s, 0, 0)),
            pl.BlockSpec((1, 8, 128), lambda s: (s, 0, 0)),
        ],
        out_specs=pl.BlockSpec((1, rows, rank), lambda s: (s, 0, 0)),
        out_shape=jax.ShapeDtypeStruct(back.shape, jnp.bfloat16),
        cost_estimate=pl.CostEstimate(
            flops=4 * count * rows * rank * rank,
            bytes_accessed=4 * count * rows * rank + 4 * count * rank * rank,
            transcendentals=0,
        ),
    )(back, factor, scales)


def update_kernel(parts, part_rows, direction_ref, basis_ref, weight_ref, out_ref):
    for part in range(parts):
        rows = pl.ds(part * part_rows, part_rows)
        update = lax.dot_general(
            direction_ref[part],
            basis_ref[0],
            (((1,), (1,)), ((), ())),
            preferred_element_type=jnp.float32,
        )
        weight = weight_ref[0, rows, :].astype(jnp.float32)
        out_ref[0, rows, :] = (0.99 * weight + update).astype(out_ref.dtype)


def row_block(rows):
    for block in (1024, 1000, 800, 512, 500, 400, 256, 200, 128, 64, 32, 16, 8):
        if rows % block == 0:
            return block
    return rows


def aligned(part_rows):
    return part_rows % 8 == 0


def apply_update(gathered, offset, part_rows, basis, weight):
    count, rows, cols = weight.shape
    tensor_size, _, rank = gathered.shape
    if aligned(part_rows):
        parts = tensor_size if tensor_size * part_rows <= 1024 else 1
        grid = (count, tensor_size // parts)
        first = offset // part_rows
        direction = gathered
        direction_spec = pl.BlockSpec(
            (parts, part_rows, rank), lambda s, i: (i, first + s, 0)
        )
        block = parts * part_rows
    else:
        piece = gathered[:, offset:offset + count * part_rows]
        piece = piece.reshape(tensor_size, count, part_rows, rank)
        direction = jnp.moveaxis(piece, 0, 1).reshape(count, rows, rank)
        parts = 1
        block = row_block(rows)
        part_rows = block
        grid = (count, rows // block)
        direction_spec = pl.BlockSpec((1, block, rank), lambda s, i: (s, i, 0))
    return pl.pallas_call(
        functools.partial(update_kernel, parts, part_rows),
        grid=grid,
        in_specs=[
            direction_spec,
            pl.BlockSpec((1, cols, rank), lambda s, i: (s, 0, 0)),
            pl.BlockSpec((1, block, cols), lambda s, i: (s, i, 0)),
        ],
        out_specs=pl.BlockSpec((1, block, cols), lambda s, i: (s, i, 0)),
        out_shape=jax.ShapeDtypeStruct(weight.shape, weight.dtype),
        cost_estimate=pl.CostEstimate(
            flops=2 * count * rows * cols * rank,
            bytes_accessed=4 * count * rows * cols + 2 * count * (rows + cols) * rank,
            transcendentals=0,
        ),
    )(direction, basis, weight)


def adam_moments(first, second, projected):
    first_new = 0.9 * first + 0.1 * projected
    second_new = 0.999 * second + 0.001 * projected * projected
    direction = first_new / (1.0 - 0.9**10) / (jnp.sqrt(second_new / (1.0 - 0.999**10)) + 1e-08)
    return (first_new, second_new, (-2.0 * direction).astype(jnp.bfloat16))


def split_rows(flat, shapes):
    parts = []
    offset = 0
    for shape in shapes:
        size = 1
        for dim in shape:
            size *= dim
        parts.append(flat[..., offset:offset + size].reshape(flat.shape[:-1] + shape))
        offset += size
    return parts


def refresh(tensor_size, groups):
    weights = [group[0] for group in groups]
    grads = [group[1] for group in groups]
    firsts = [group[2] for group in groups]
    seconds = [group[3] for group in groups]
    olds = [group[4] for group in groups]
    counts = [grad.shape[0] for grad in grads]
    sketch_terms = [
        jnp.einsum("smc,scr->smr", grad, old, preferred_element_type=jnp.float32).astype(jnp.bfloat16)
        for grad, old in zip(grads, olds)
    ]
    sketches = lax.psum(tuple(sketch_terms), "tensor")
    back_terms = [
        jnp.einsum("smc,smr->scr", grad, sketch, preferred_element_type=jnp.float32)
        for grad, sketch in zip(grads, sketches)
    ]
    back_all = jnp.concatenate(back_terms, axis=0).astype(jnp.bfloat16)
    backs = lax.psum(back_all, "shard")
    grams = symmetric_psum(local_gram(backs), "tensor")
    basis_all = polish_small(backs, grams)
    bases = []
    offset = 0
    for count in counts:
        bases.append(basis_all[offset:offset + count])
        offset += count
    proj_parts = []
    row_shapes = []
    for grad, basis in zip(grads, bases):
        count, rows, cols = grad.shape
        split = grad.reshape(count, tensor_size, rows // tensor_size, cols)
        proj = jnp.einsum("sjmc,scr->jsmr", split, basis, preferred_element_type=jnp.float32)
        row_shapes.append((count, rows // tensor_size, basis.shape[2]))
        proj_parts.append(proj.reshape(tensor_size, -1, basis.shape[2]).astype(jnp.bfloat16))
    proj_all = jnp.concatenate(proj_parts, axis=1)
    proj_mine = lax.psum_scatter(proj_all, "tensor", scatter_dimension=0, tiled=True).reshape(-1)
    projected = [part.astype(jnp.float32) for part in split_rows(proj_mine, row_shapes)]
    results = [
        adam_moments(first, second, proj) for first, second, proj in zip(firsts, seconds, projected)
    ]
    order = sorted(range(len(results)), key=lambda index: -row_shapes[index][1])
    offsets = [0] * len(results)
    pieces = []
    cursor = 0
    for index in order:
        count, part_rows, rank = row_shapes[index]
        start = cursor
        if aligned(part_rows):
            start = -(-cursor // part_rows) * part_rows
        if start > cursor:
            pieces.append(jnp.zeros((start - cursor, rank), jnp.bfloat16))
        pieces.append(results[index][2].reshape(count * part_rows, rank))
        offsets[index] = start
        cursor = start + count * part_rows
    dir_all = jnp.concatenate(pieces, axis=0)
    gathered = lax.all_gather(dir_all, "tensor", axis=0, tiled=False)
    outputs = []
    for index, (weight, basis, result) in enumerate(zip(weights, bases, results)):
        part_rows = row_shapes[index][1]
        weight_new = apply_update(gathered, offsets[index], part_rows, basis, weight)
        outputs.append((weight_new, result[0], result[1]))
    return outputs


def per_device(tensor_size, *arrays):
    wide, narrow, vocab = arrays[0:5], arrays[5:10], arrays[10:15]
    wide_out, narrow_out, vocab_out = refresh(tensor_size, [wide, narrow, vocab])
    return tuple(wide_out) + tuple(narrow_out) + tuple(vocab_out)


def solution(mesh):
    in_specs = (
        P(None, "shard", "tensor"),
        P(None, "shard", "tensor"),
        P(None, ("shard", "tensor"), None),
        P(None, ("shard", "tensor"), None),
        P(None, "tensor", None),
        P(None, "shard", "tensor"),
        P(None, "shard", "tensor"),
        P(None, ("shard", "tensor"), None),
        P(None, ("shard", "tensor"), None),
        P(None, "tensor", None),
        P(None, "shard", "tensor"),
        P(None, "shard", "tensor"),
        P(None, ("shard", "tensor"), None),
        P(None, ("shard", "tensor"), None),
        P(None, "tensor", None),
    )
    out_specs = (
        P(None, "shard", "tensor"),
        P(None, ("shard", "tensor"), None),
        P(None, ("shard", "tensor"), None),
        P(None, "shard", "tensor"),
        P(None, ("shard", "tensor"), None),
        P(None, ("shard", "tensor"), None),
        P(None, "shard", "tensor"),
        P(None, ("shard", "tensor"), None),
        P(None, ("shard", "tensor"), None),
    )
    return jax.shard_map(
        functools.partial(per_device, mesh.shape["tensor"]), mesh=mesh, in_specs=in_specs, out_specs=out_specs, check_vma=False
    )
```

time: 654 us -> 597 us (0.913)
  matrix products: 120 us -> 73.9 us
  Pallas kernels: 0 us -> 39.6 us
  other arithmetic: 45.9 us -> 17.2 us
  waiting for transfers between devices: 445 us -> 429 us
    dot_general x22 -> x17, matrix products: 113 us -> 69.9 us  [the longest x3 20.2 us: refresh(): jnp.einsum('smc,scr->smr', grad, old, preferred_element_type=jnp.float32)]
    pallas_call x0 -> x4, Pallas kernels: none -> 39.6 us  [the longest x3 29.3 us: apply_update(): pl.pallas_call(functools.partial(update_kernel, parts, part_rows), grid=g...]
    convert_element_type x7 -> x3, other arithmetic: 36.7 us -> 5.7 us  [adam_moments(): return (first_new, second_new, (-2.0 * direction).astype(jnp.bfloat16))]
    psum x3, waiting for transfers between devices: 351 us -> 341 us  [the longest x1 184 us: refresh(): backs = lax.psum(back_all, 'shard')]
    slice x0 -> x4, local copies, waits for them, and re-layouts: none -> 8.88 us  [the longest x2 6.84 us: refresh(): bases.append(basis_all[offset:offset + count])]
    unnamed x52 -> x32, local copies, waits for them, and re-layouts: 9 us -> 1.34 us
    all_gather x1 -> x0, local copies, waits for them, and re-layouts: 6.94 us -> none  [per_device(): dir_gathered = lax.all_gather(dir_all, 'tensor', axis=0, tiled=False)]
  transfers between devices with their start and end apart: 5 -> 5, of which waited for: 5 -> 5; matrix products, arithmetic and copies ran while one was open for 0% -> 1% of each run, Pallas kernels for 0% -> 0%
where the time goes in v3:
time: 597 us; the launch traced here: 591 us
  waiting for transfers between devices  429 us (72%)
  matrix products  73.9 us (12%)
  Pallas kernels  39.6 us (7%)
  other arithmetic  17.2 us (3%)
  local copies, waits for them, and re-layouts  16.8 us (3%)
  between operations  14.5 us (2%)
    psum x1, waiting for transfers between devices, refresh(): backs = lax.psum(back_all, 'shard')  184 us
    psum x1, waiting for transfers between devices, refresh(): sketches = lax.psum(tuple(sketch_terms), 'tensor')  108 us
    reduce_scatter x1, waiting for transfers between devices, refresh(): lax.psum_scatter(proj_all, 'tensor', scatter_dimension=0, tiled=True)  52.5 us
    psum x1, waiting for transfers between devices, symmetric_psum(): top, corner = lax.psum((gram[:, :half, :], gram[:, half:, half:]), axis)  48.5 us
    all_gather x1, waiting for transfers between devices, refresh(): gathered = lax.all_gather(dir_all, 'tensor', axis=0, tiled=False)  35.2 us
    pallas_call x3, Pallas kernels, apply_update(): pl.pallas_call(functools.partial(update_kernel, parts, part_rows), grid=g...  29.3 us
    dot_general x3, matrix products, refresh(): jnp.einsum('smc,scr->smr', grad, old, preferred_element_type=jnp.float32)  20.2 us
    dot_general x3, matrix products, refresh(): jnp.einsum('smc,smr->scr', grad, sketch, preferred_element_type=jnp.float32)  16 us
  transfers between devices with their start and end apart: 5, of which 5 were waited for; matrix products, arithmetic and copies ran while one was open for 1% of the time, Pallas kernels for 0%

profile of v3, /device:TPU:0, one launch (start us, length us, event | category | flops | bytes accessed | tf_op | source)
XLA Modules:
  0.0 591.2 jit_solution(1586049194433237081)
XLA Ops:
  7.2 3.6 convolution_convert_fusion.3
  10.9 4.5 convolution_convert_fusion.2
  15.4 12.1 %convolution_convert_fusion = bf16[2,4000,256]{2,1,0:T(8,128)(2,1)} fusion(bf16[2,4000,1024]{2,1,0:T(8,128)(2,1)} %param.26, bf16[2,1024,256]{2,1,0:T(8,128)(2,1)S(1)} %copy-done.15), kind=kOutput, calls=%fused_computation | convolution fusion | flops 4196352000 | bytes 21528576 | tf_op jit(solution)/shard_map/smc,scr->smr/dot_general | solution.py:172
  27.7 108.2 %all-reduce.10.cloned.1.call-done = (bf16[2,4000,256]{2,1,0:T(8,128)(2,1)}, bf16[4,128,256]{1,2,0:T(8,128)(2,1)}, bf16[4,512,256]{1,2,0:T(8,128)(2,1)}) async-done(((bf16[2,4000,256]{2,1,0:T(8,128)(2,1)}, bf16[4,128,256]{1,2,0:T(8,128)(2,1)}, bf16[4,512,256]{1,2,0:T(8,128)(2,1)}), (bf16[2,4000,256]{2,1,0:T(8,128)(2,1)}, bf16[4,128,256]{1,2,0:T(8,128)(2,1)}, ...) | async-done | bytes 5406736 | tf_op jit(solution)/shard_map/psum | solution.py:175
  135.9 11.4 %fusion.33 = bf16[2,1024,256]{2,1,0:T(8,128)(2,1)S(1)} fusion(bf16[2,4000,256]{2,1,0:T(8,128)(2,1)} %get-tuple-element.11, bf16[2,4000,1024]{2,1,0:T(8,128)(2,1)} %param.26), kind=kOutput, calls=%fused_computation.46 | convolution fusion | flops 4194828288 | bytes 21528576 | tf_op jit(solution)/shard_map/smc,smr->scr/dot_general | solution.py:177
  148.6 3.8 convert_bitcast_fusion.2
  152.4 2.9 pad_maximum_fusion.1
  155.3 184.3 %all-reduce.6.cloned.1.call-done.back_ref = bf16[10,1024,256]{2,1,0:T(8,128)(2,1)} async-done(((bf16[10,1024,256]{2,1,0:T(8,128)(2,1)}), bf16[10,1024,256]{2,1,0:T(8,128)(2,1)}) %all-reduce.6.cloned.1.call-update) | async-done | bytes 5242896 | tf_op jit(solution)/shard_map/psum | solution.py:181
  339.6 5.7 fusion.91
  347.5 48.5 %all-reduce.8.cloned.1.call-done = (f32[10,128,128]{2,1,0:T(8,128)}, f32[10,128,256]{2,1,0:T(8,128)}) async-done(((f32[10,128,128]{2,1,0:T(8,128)}, f32[10,128,256]{2,1,0:T(8,128)}), (f32[10,128,128]{2,1,0:T(8,128)}, f32[10,128,256]{2,1,0:T(8,128)})) %all-reduce.8.cloned.1.call-update) | async-done | bytes 1966096 | tf_op jit(solution)/shard_map/psum | solution.py:22
  415.3 3.2 fusion.factor_ref
  419.2 10.3 %shard_map.214 = bf16[10,1024,256]{2,1,0:T(8,128)(2,1)} custom-call(bf16[10,1024,256]{2,1,0:T(8,128)(2,1)} %all-reduce.6.cloned.1.call-done.back_ref, f32[10,256,256]{2,1,0:T(8,128)} %fusion.factor_ref, f32[10,8,128]{2,1,0:T(8,128)} %broadcast_in_dim.19.scale_ref), custom_call_target="tpu_custom_call" | custom-call | flops 2684354560 | bytes 13107200 | tf_op jit(solution)/shard_map/pallas_call | solution.py:64
  432.3 2.9 fusion.30
  435.3 8.3 %convert_bitcast_fusion = bf16[4,2,1000,256]{3,2,0,1:T(8,128)(2,1)S(1)} fusion(bf16[2,4,1000,1024]{3,2,1,0:T(8,128)(2,1)} %bitcast.92, bf16[10,1024,256]{2,1,0:T(8,128)(2,1)} %shard_map.214), kind=kOutput, calls=%fused_computation.3 | convolution fusion | flops 4196352000 | bytes 21528576 | tf_op jit(solution)/shard_map/sjmc,scr->jsmr/dot_general | solution.py:194
  443.9 2.8 pad_maximum_fusion
  446.8 52.5 %reduce-scatter.2.cloned.1.call-done = bf16[1,2640,256]{2,1,0:T(8,128)(2,1)} async-done(((bf16[4,2640,256]{2,1,0:T(8,128)(2,1)}), bf16[1,2640,256]{2,1,0:T(8,128)(2,1)}) %reduce-scatter.2.cloned.1.call-update) | async-done | bytes 1351696 | tf_op jit(solution)/shard_map/reduce_scatter | solution.py:198
  503.8 3.6 multiply_convert_fusion
  507.3 5.4 pad_maximum_fusion.2
  512.8 2.3 slice.44.basis_ref
  515.1 4.5 fusion.90
  519.6 35.2 %all-gather.3.cloned.1.call-done = bf16[10752,256]{1,0:T(8,128)(2,1)} async-done(((bf16[2688,256]{1,0:T(8,128)(2,1)}), bf16[10752,256]{1,0:T(8,128)(2,1)}) %all-gather.3.cloned.1.call-update) | async-done | bytes 5505040 | tf_op jit(solution)/shard_map/all_gather | solution.py:218
  554.9 5.3 shard_map.216
  560.2 7.0 %shard_map.215 = bf16[4,512,1024]{2,1,0:T(8,128)(2,1)} custom-call(bf16[4,2688,256]{2,1,0:T(8,128)(2,1)} %bitcast.79, bf16[4,1024,256]{2,1,0:T(8,128)(2,1)} %get-tuple-element.24.basis_ref, bf16[4,512,1024]{2,1,0:T(8,128)(2,1)} %weight_ref.3), custom_call_target="tpu_custom_call" | custom-call | flops 1073741824 | bytes 11534336 | tf_op jit(solution)/shard_map/pallas_call | solution.py:127
  567.2 16.9 %shard_map.217 = bf16[2,4000,1024]{2,1,0:T(8,128)(2,1)} custom-call(bf16[4,2688,256]{2,1,0:T(8,128)(2,1)} %bitcast.80, bf16[2,1024,256]{2,1,0:T(8,128)(2,1)} %slice.44.basis_ref, bf16[2,4000,1024]{2,1,0:T(8,128)(2,1)} %weight_ref.5), custom_call_target="tpu_custom_call" | custom-call | flops 4194304000 | bytes 37912576 | tf_op jit(solution)/shard_map/pallas_call | solution.py:127
  (72 shorter events, 31.3 us)
Async XLA Ops:
  7.2 3.7 copy-start
  7.2 128.7 %all-reduce.10.cloned.1.call-start = ((), (), s32[]{:S(2)}) async-start(), calls=%async_computation.5 | async-start | bytes 10813440 | tf_op jit(solution)/shard_map/psum | solution.py:175
  10.9 4.5 copy-start.15
  27.5 312.1 %all-reduce.6.cloned.1.call-start = ((), (), s32[]{:S(2)}) async-start(), calls=%async_computation.1 | async-start | bytes 10485760 | tf_op jit(solution)/shard_map/psum | solution.py:181
  135.9 11.4 %copy-start.5 = (bf16[4,128,1024]{2,1,0:T(8,128)(2,1)S(1)}, bf16[4,128,1024]{2,1,0:T(8,128)(2,1)}, u32[]{:S(2)}) copy-start(bf16[4,128,1024]{2,1,0:T(8,128)(2,1)} %param.21) | copy-start | bytes 3145732
  135.9 11.4 %copy-start.12 = (bf16[4,128,256]{1,2,0:T(8,128)(2,1)S(1)}, bf16[4,128,256]{1,2,0:T(8,128)(2,1)}, u32[]{:S(2)}) copy-start(bf16[4,128,256]{1,2,0:T(8,128)(2,1)} %get-tuple-element.12) | copy-start | bytes 786436
  147.3 1.2 copy-start.9
  155.3 240.7 %all-reduce.8.cloned.1.call-start = ((), (), s32[]{:S(2)}) async-start(), calls=%async_computation.4 | async-start | bytes 3932160 | tf_op jit(solution)/shard_map/psum | solution.py:22
  347.4 152.0 %reduce-scatter.2.cloned.1.call-start = ((), (), s32[]{:S(2)}) async-start(), calls=%async_computation.2 | async-start | bytes 6758400 | tf_op jit(solution)/shard_map/reduce_scatter | solution.py:198
  396.0 3.4 copy-start.2
  396.0 3.5 copy-start.3
  419.2 10.3 %copy-start.6 = (bf16[4,128,1024]{2,1,0:T(8,128)(2,1)S(1)}, bf16[4,128,1024]{2,1,0:T(8,128)(2,1)}, u32[]{:S(2)}) copy-start(bf16[4,128,1024]{2,1,0:T(8,128)(2,1)} %param.21) | copy-start | bytes 3145732
  429.5 2.8 copy-start.4
  446.7 53.5 %copy-start.13 = (f32[4,32,256]{2,1,0:T(8,128)S(1)}, f32[4,32,256]{2,1,0:T(8,128)}, u32[]{:S(2)}) copy-start(f32[4,32,256]{2,1,0:T(8,128)} %param.22) | copy-start | bytes 393220
  446.7 53.5 %copy-start.14 = (f32[4,32,256]{2,1,0:T(8,128)S(1)}, f32[4,32,256]{2,1,0:T(8,128)}, u32[]{:S(2)}) copy-start(f32[4,32,256]{2,1,0:T(8,128)} %param.23) | copy-start | bytes 393220
  446.7 55.5 %copy-start.10 = (f32[4,128,256]{2,1,0:T(8,128)S(1)}, f32[4,128,256]{2,1,0:T(8,128)}, u32[]{:S(2)}) copy-start(f32[4,128,256]{2,1,0:T(8,128)} %param.17) | copy-start | bytes 1572868
  446.7 55.5 %copy-start.11 = (f32[4,128,256]{2,1,0:T(8,128)S(1)}, f32[4,128,256]{2,1,0:T(8,128)}, u32[]{:S(2)}) copy-start(f32[4,128,256]{2,1,0:T(8,128)} %param.18) | copy-start | bytes 1572868
  446.7 108.2 %all-gather.3.cloned.1.call-start = ((), (), s32[]{:S(2)}) async-start(), calls=%async_computation.3 | async-start | bytes 6881280 | tf_op jit(solution)/shard_map/all_gather | solution.py:218
  501.0 2.5 slice-start
  501.0 2.5 copy-start.7
  501.0 2.8 copy-start.8
  567.2 16.9 %copy-start.1 = (bf16[4,1024,256]{2,1,0:T(8,128)(2,1)S(1)}, bf16[4,1024,256]{2,1,0:T(8,128)(2,1)}, u32[]{:S(2)}) copy-start(bf16[4,1024,256]{2,1,0:T(8,128)(2,1)} %param.19) | copy-start | bytes 6291460
Sparse Core Ops, SparseCore 0:
  27.6 108.2 all-reduce.9
  155.4 184.1 all-reduce.5
  347.5 48.4 all-reduce.7
  446.8 52.4 reduce-scatter.1
  512.9 41.9 all-gather.2
